TPU v7x, 32 devices: a whole 2x2x4 slice. The times are simulated.
32 devices in a mesh: groups: 2 (over x), height: 16 (over z, y, core).
Axes of the slice: x: 2, y: 2, z: 4, core: 2. Of those that a mesh axis runs over, the one named last changes fastest.
Arguments:
- latent: bfloat16 [3, 64, 80, 512], P(None, ('groups', 'height')), parts along dimension 1, may hold values from -120 to 120
- gain_first: float32 [512], replicated, may hold values from 0.1 to 1.9
- shift_first: float32 [512], replicated, may hold values from -3 to 3
- kernel_first: bfloat16 [27, 512, 512], P(None, 'height'), may hold values from -0.0546875 to 0.0546875
- bias_first: float32 [512], replicated, may hold values from -2 to 2
- gain_second: float32 [512], replicated, may hold values from 0.1 to 1.9
- shift_second: float32 [512], replicated, may hold values from -3 to 3
- kernel_second: bfloat16 [27, 512, 512], P(None, 'height'), may hold values from -0.0546875 to 0.0546875
- bias_second: float32 [512], replicated, may hold values from -2 to 2
Outputs:
- upsampled: bfloat16 [3, 128, 160, 512], P(None, ('groups', 'height')), parts along dimension 1
There are 2 independent parts, one for each index of `groups`. A program takes and returns all parts, laid end to end along the dimension named above; an argument that names none is the same for every part. Nothing has to cross between parts.
All inputs are finite; a program needn't handle non-finite values.
Results may differ from a plain program's by a relative error of at most 0.0045.
Values may be sent and summed in bfloat16 or wider, within the bound.
No kernel may reach another device: no remote copies, remote signals or barrier semaphores. Data moves between devices by JAX's collectives and lax.ppermute only.
A program may use at most 128 MiB of HBM per device.

v0:
```python
import jax
import jax.numpy as jnp
from jax import lax
from jax.sharding import PartitionSpec as P

GROUPS = 32


def with_halo(cells, sides, width):
    for axis, dim in sides:
        count = lax.axis_size(axis)
        ends = count - 1
        head = lax.slice_in_dim(cells, 0, width, axis=dim)
        tail = lax.slice_in_dim(cells, cells.shape[dim] - width, cells.shape[dim], axis=dim)
        cells = jnp.concatenate(
            [
                lax.ppermute(tail, axis, [(i, (i + 1) % count) for i in range(ends)]),
                cells,
                lax.ppermute(head, axis, [((i + 1) % count, i) for i in range(ends)]),
            ],
            axis=dim,
        )
    return cells


def moments(field, cells):
    values = field.astype(jnp.float32)
    chan_total = values.shape[3]
    group_size = chan_total // GROUPS
    chan_sums = jnp.sum(values, axis=(0, 1, 2)).reshape(GROUPS, group_size).sum(axis=1)
    squares = jnp.sum(values * values, axis=(0, 1, 2)).reshape(GROUPS, group_size).sum(axis=1)
    summed, spread = lax.psum((chan_sums, squares), "height")
    group_mean = summed / cells
    variance = spread / cells - group_mean * group_mean
    mean_chan = jnp.repeat(group_mean, group_size)
    scale_chan = jnp.repeat(lax.rsqrt(variance + 1e-06), group_size)
    return (mean_chan, scale_chan)


def activate(field, mean_chan, scale_chan, norm_gain, norm_shift):
    values = field.astype(jnp.float32)
    normed = (values - mean_chan) * scale_chan * norm_gain + norm_shift
    return jax.nn.silu(normed).astype(jnp.bfloat16)


def pad_local(extended):
    leading = jnp.concatenate([extended[:1], extended[:1], extended], axis=0)
    return jnp.pad(leading, ((0, 0), (0, 0), (1, 1), (0, 0)))


def tap_sum(padded, kernel_part, out_rows):
    frame_total = padded.shape[0] - 2
    col_total = padded.shape[2] - 2
    summed = jnp.zeros((frame_total, out_rows, col_total, kernel_part.shape[2]), jnp.float32)
    for step_t in range(3):
        for step_h in range(3):
            for step_w in range(3):
                window = padded[
                    step_t : step_t + frame_total,
                    step_h : step_h + out_rows,
                    step_w : step_w + col_total,
                ]
                summed = summed + jnp.einsum(
                    "fhwk,ko->fhwo",
                    window,
                    kernel_part[9 * step_t + 3 * step_h + step_w],
                    preferred_element_type=jnp.float32,
                )
    return summed


def convolve(padded, kernel, out_rows):
    gathered = lax.all_gather(kernel, "height", axis=1, tiled=True)
    return tap_sum(padded, gathered, out_rows)


def per_device(
    latent,
    gain_first,
    shift_first,
    kernel_first,
    bias_first,
    gain_second,
    shift_second,
    kernel_second,
    bias_second,
):
    frame_total, slab_rows, col_total, chan_total = latent.shape
    slab_count = lax.axis_size("height")
    cells = float(frame_total * slab_rows * slab_count * col_total * (chan_total // GROUPS))
    mean_chan, scale_chan = moments(latent, cells)
    act_first = activate(latent, mean_chan, scale_chan, gain_first, shift_first)
    extended = with_halo(act_first, (("height", 1),), 1)
    hidden = (convolve(pad_local(extended), kernel_first, slab_rows) + bias_first).astype(
        jnp.bfloat16
    )
    mean_next, scale_next = moments(hidden, cells)
    act_second = activate(hidden, mean_next, scale_next, gain_second, shift_second)
    extended_next = with_halo(act_second, (("height", 1),), 1)
    branch = convolve(pad_local(extended_next), kernel_second, slab_rows) + bias_second
    summed = (latent.astype(jnp.float32) + branch).astype(jnp.bfloat16)
    return jnp.repeat(jnp.repeat(summed, 2, axis=1), 2, axis=2)


def solution(mesh):
    placed = (
        P(None, ("groups", "height"), None, None),
        P(),
        P(),
        P(None, "height", None),
        P(),
        P(),
        P(),
        P(None, "height", None),
        P(),
    )
    return jax.shard_map(
        per_device,
        mesh=mesh,
        in_specs=placed,
        out_specs=P(None, ("groups", "height"), None, None),
        check_vma=False,
    )
```

profile of v0, /device:TPU:0, one launch (start us, length us, event | category | flops | bytes accessed | tf_op | source)
XLA Modules:
  0.0 292.4 jit_solution(4379032982951424562)
XLA Ops:
  8.6 36.1 %all-reduce.3 = (f32[32]{0:T(128)S(1)}, f32[32]{0:T(128)S(1)}) all-reduce(f32[32]{0:T(128)S(1)} %reduce_sum.75, f32[32]{0:T(128)S(1)} %reduce_sum.73), channel_id=1, replica_groups=mesh['groups'=2,'height'=16] {'height'}, use_global_device_ids=true, to_apply=%region_5.0 | all-reduce | flops 64 | bytes 512 | tf_op jit(solution)/shard_map/psum | solution.py:32
  48.0 2.1 collective-permute-done.1
  50.3 75.3 %all-gather.3.cloned.1.call-done = bf16[27,512,512]{2,1,0:T(8,128)(2,1)} async-done(((bf16[27,32,512]{2,1,0:T(8,128)(2,1)}), bf16[27,512,512]{2,1,0:T(8,128)(2,1)}) %all-gather.3.cloned.1.call-update) | async-done | bytes 14155792 | tf_op jit(solution)/shard_map/all_gather | solution.py:73
  125.7 2.6 fusion.77
  128.2 3.2 %fusion.80 = f32[3,2,80,512]{3,2,1,0:T(8,128)} fusion(bf16[27,512,512]{2,1,0:T(8,128)(2,1)} %all-gather.3.cloned.1.call-done, bf16[3,1,80,512]{3,2,1,0:T(8,128)(2,1)S(1)} %collective-permute-done.1, bf16[3,2,80,512]{3,2,1,0:T(8,128)(2,1)S(1)} %fusion.28, bf16[3,1,80,512]{3,2,1,0:T(8,128)(2,1)S(1)} %collective-permute-done, ...), kind=kOutput, calls=%fused_computation.134 | convolution fusion | flops 256901120 | bytes 2818048 | tf_op jit(solution)/shard_map/fhwk,ko->fhwo/dot_general | solution.py:63
  131.5 2.4 fusion.83
  133.9 1.5 fusion.71
  140.2 1.4 fusion.85
  141.6 1.4 fusion.87
  143.0 1.4 fusion.88
  144.4 1.4 fusion.90
  152.7 1.4 fusion.72
  154.1 1.4 fusion.86
  156.9 1.4 fusion.92
  158.3 6.9 %convert_reduce_fusion.1 = (f32[512]{0:T(512)S(1)}, f32[512]{0:T(512)S(1)}, bf16[3,2,80,512]{3,2,1,0:T(8,128)(2,1)S(1)}) fusion(f32[512]{0:T(512)S(1)} %copy-done.4, f32[3,2,80,512]{3,2,1,0:T(8,128)} %fusion.70, f32[3,2,80,512]{3,2,1,0:T(8,128)} %fusion.34, f32[3,2,80,512]{3,2,1,0:T(8,128)S(1)} %fusion.71, bf16[27,512,512]{2,1,0:T(8,128)(2,1)S(1)} %copy-done.1, ...), kind=kOutput, calls=%fused_computation.8 | convolution fusion | flops 259521536 | bytes 28219392 | tf_op jit(solution)/shard_map/fhwk,ko->fhwo/dot_general | solution.py:63
  165.7 31.7 %all-reduce.2 = (f32[32]{0:T(128)S(1)}, f32[32]{0:T(128)S(1)}) all-reduce(f32[32]{0:T(128)S(1)} %reduce_sum.79, f32[32]{0:T(128)S(1)} %reduce_sum.77), channel_id=1, replica_groups=mesh['groups'=2,'height'=16] {'height'}, use_global_device_ids=true, to_apply=%region_11.12 | all-reduce | flops 64 | bytes 512 | tf_op jit(solution)/shard_map/psum | solution.py:32
  199.4 1.5 collective-permute-start.3
  200.9 41.7 %all-gather.5.cloned.1.call-done = bf16[27,512,512]{2,1,0:T(8,128)(2,1)} async-done(((bf16[27,32,512]{2,1,0:T(8,128)(2,1)}), bf16[27,512,512]{2,1,0:T(8,128)(2,1)}) %all-gather.5.cloned.1.call-update) | async-done | bytes 14155792 | tf_op jit(solution)/shard_map/all_gather | solution.py:73
  242.6 1.6 fusion.48
  244.2 2.8 fusion.59
  247.1 2.6 fusion.56
  249.7 2.4 fusion.53
  252.1 1.4 fusion.38
  259.4 1.4 fusion.61
  263.5 1.4 fusion.64
  264.9 1.4 fusion.65
  267.7 1.5 fusion.67
  269.2 1.4 fusion.68
  270.6 1.4 fusion.69
  273.4 7.4 %fusion.8 = bf16[3,2,80,512]{3,2,1,0:T(8,128)(2,1)} fusion(f32[3,2,80,512]{3,2,1,0:T(8,128)} %fusion.46, f32[3,2,80,512]{3,2,1,0:T(8,128)} %fusion.42, f32[3,2,80,512]{3,2,1,0:T(8,128)S(1)} %fusion.47, bf16[3,2,80,512]{3,2,1,0:T(8,128)(2,1)S(1)} %copy-done.2, f32[3,2,80,512]{3,2,1,0:T(8,128)S(1)} %fusion.48, f32[3,2,80,512]{3,2,1,0:T(8,128)S(1)} %fusion.49, ...), kind=kOutput, calls=%fused_computation.21 | convolution fusion | flops 259031040 | bytes 28706816 | tf_op jit(solution)/shard_map/fhwk,ko->fhwo/dot_general | solution.py:63
  281.9 1.4 broadcast_in_dim.29
  283.4 2.2 reshape.33
  (88 shorter events, 33.5 us)
Async XLA Ops:
  6.5 1.5 copy-start.2
  6.5 38.4 %copy-start.7 = (f32[512]{0:T(512)S(1)}, f32[512]{0:T(512)}, u32[]{:S(2)}) copy-start(f32[512]{0:T(512)} %param.10) | copy-start | bytes 6148
  6.5 38.5 %copy-start.6 = (f32[512]{0:T(512)S(1)}, f32[512]{0:T(512)}, u32[]{:S(2)}) copy-start(f32[512]{0:T(512)} %param.11) | copy-start | bytes 6148
  6.5 119.1 %all-gather.3.cloned.1.call-start = ((), (), s32[]{:S(2)}) async-start(), calls=%async_computation | async-start | bytes 15040512 | tf_op jit(solution)/shard_map/all_gather | solution.py:73
  7.3 235.3 %all-gather.5.cloned.1.call-start = ((), (), s32[]{:S(2)}) async-start(), calls=%async_computation.1 | async-start | bytes 15040512 | tf_op jit(solution)/shard_map/all_gather | solution.py:73
  45.4 2.6 collective-permute-start
  46.7 3.4 %collective-permute-start.1 = (bf16[3,1,80,512]{3,2,1,0:T(8,128)(2,1)S(1)}, bf16[3,1,80,512]{3,2,1,0:T(8,128)(2,1)S(1)}, u32[]{:S(2)}, u32[]{:S(2)}) collective-permute-start(bf16[3,1,80,512]{3,2,1,0:T(8,128)(2,1)S(1)} %get-tuple-element.16), channel_id=1, source_target_pairs={{1,0},{2,1},{3,2},{4,3},{5,4},{6,5},{7,6},{8,7},{9,8},{10,9},{11,1... | collective-permute-start | bytes 737288 | tf_op jit(solution)/shard_map/ppermute | solution.py:19
  125.7 9.7 %copy-start.1 = (bf16[27,512,512]{2,1,0:T(8,128)(2,1)S(1)}, bf16[27,512,512]{2,1,0:T(8,128)(2,1)}, u32[]{:S(2)}) copy-start(bf16[27,512,512]{2,1,0:T(8,128)(2,1)} %all-gather.3.cloned.1.call-done) | copy-start | bytes 42467332
  155.5 2.8 copy-start.3
  155.5 2.8 copy-start.4
  158.3 39.4 %copy-start.8 = (f32[512]{0:T(512)S(1)}, f32[512]{0:T(512)}, u32[]{:S(2)}) copy-start(f32[512]{0:T(512)} %param.15) | copy-start | bytes 6148
  158.3 39.4 %copy-start.9 = (f32[512]{0:T(512)S(1)}, f32[512]{0:T(512)}, u32[]{:S(2)}) copy-start(f32[512]{0:T(512)} %param.14) | copy-start | bytes 6148
  198.1 46.1 %collective-permute-start.2 = (bf16[3,1,80,512]{3,2,1,0:T(8,128)(2,1)S(1)}, bf16[3,1,80,512]{3,2,1,0:T(8,128)(2,1)S(1)}, u32[]{:S(2)}, u32[]{:S(2)}) collective-permute-start(bf16[3,1,80,512]{3,2,1,0:T(8,128)(2,1)S(1)} %get-tuple-element.13), channel_id=1, source_target_pairs={{0,1},{1,2},{2,3},{3,4},{4,5},{5,6},{6,7},{7,8},{8,9},{9,10},{10,1... | collective-permute-start | bytes 737288 | tf_op jit(solution)/shard_map/ppermute | solution.py:17
  199.4 44.8 %collective-permute-start.3 = (bf16[3,1,80,512]{3,2,1,0:T(8,128)(2,1)S(1)}, bf16[3,1,80,512]{3,2,1,0:T(8,128)(2,1)S(1)}, u32[]{:S(2)}, u32[]{:S(2)}) collective-permute-start(bf16[3,1,80,512]{3,2,1,0:T(8,128)(2,1)S(1)} %get-tuple-element.14), channel_id=1, source_target_pairs={{1,0},{2,1},{3,2},{4,3},{5,4},{6,5},{7,6},{8,7},{9,8},{10,9},{11,1... | collective-permute-start | bytes 737288 | tf_op jit(solution)/shard_map/ppermute | solution.py:19
  242.6 9.6 %copy-start = (bf16[27,512,512]{2,1,0:T(8,128)(2,1)S(1)}, bf16[27,512,512]{2,1,0:T(8,128)(2,1)}, u32[]{:S(2)}) copy-start(bf16[27,512,512]{2,1,0:T(8,128)(2,1)} %all-gather.5.cloned.1.call-done) | copy-start | bytes 42467332
  272.0 1.4 copy-start.5
Sparse Core Ops, SparseCore 0:
  9.5 116.0 all-gather.2
  127.9 114.6 all-gather.4
where the time goes:
time: 293 us; the launch traced here: 292 us
  waiting for transfers between devices  121 us (41%)
  matrix products  77.5 us (26%)
  blocking collectives  67.8 us (23%)
  between operations  13.7 us (5%)
  local copies, waits for them, and re-layouts  5.75 us (2%)
  starting transfers between devices  5.41 us (2%)
    all_gather x2, waiting for transfers between devices, convolve(): gathered = lax.all_gather(kernel, 'height', axis=1, tiled=True)  117 us
    dot_general x54, matrix products, tap_sum(): jnp.einsum('fhwk,ko->fhwo', window, kernel_part[9 * step_t + 3 * step_h +...  77.5 us
    psum x2, blocking collectives, moments(): summed, spread = lax.psum((chan_sums, squares), 'height')  67.8 us
  transfers between devices with their start and end apart: 6, of which 3 were waited for; matrix products, arithmetic and copies ran while one was open for 15% of the time, Pallas kernels for 0%

commit v1 on v0

--- a/solution.py
+++ b/solution.py
@@ -4,6 +4,19 @@
 from jax.sharding import PartitionSpec as P
 
 GROUPS = 32
+
+
+def gather_around(x, axis, dim):
+    ways = lax.axis_size(axis)
+    up = [(d, (d + 1) % ways) for d in range(ways)]
+    down = [(d, (d - 1) % ways) for d in range(ways)]
+    earlier, later = ([x], [x])
+    for _ in range(ways // 2):
+        earlier.append(lax.ppermute(earlier[-1], axis, up))
+    for _ in range((ways - 1) // 2):
+        later.append(lax.ppermute(later[-1], axis, down))
+    line = jnp.concatenate([*earlier[::-1], *later[1:]], axis=dim)
+    return jnp.roll(line, (lax.axis_index(axis) - ways // 2) * x.shape[dim], axis=dim)
 
 
 def with_halo(cells, sides, width):
@@ -70,7 +83,7 @@
 
 
 def convolve(padded, kernel, out_rows):
-    gathered = lax.all_gather(kernel, "height", axis=1, tiled=True)
+    gathered = gather_around(kernel, "height", 1)
     return tap_sum(padded, gathered, out_rows)
 
 

time: 293 us -> 457 us (1.56)
  starting transfers between devices: 5.41 us -> 197 us
  waiting for transfers between devices: 121 us -> 56 us
  other arithmetic: 1.75 us -> 35.6 us
  matrix products: 77.5 us -> 54.1 us
  local copies, waits for them, and re-layouts: 5.75 us -> 28.8 us
  blocking collectives: 67.8 us -> 82.7 us
  between operations: 13.7 us -> 0.96 us
    ppermute x0 -> x30, starting transfers between devices: none -> 191 us  [the longest x16 126 us: gather_around(): earlier.append(lax.ppermute(earlier[-1], axis, up))]
    all_gather x2 -> x0, waiting for transfers between devices: 117 us -> none  [convolve(): gathered = lax.all_gather(kernel, 'height', axis=1, tiled=True)]
    ppermute x2, waiting for transfers between devices: 2.1 us -> 36.4 us  [with_halo(): lax.ppermute(head, axis, [((i + 1) % count, i) for i in range(ends)])]
    concatenate x0 -> x2, other arithmetic: none -> 31.7 us  [gather_around(): jnp.roll(line, (lax.axis_index(axis) - ways // 2) * x.shape[dim], axis=dim)]
    dot_general x54, matrix products: 77.5 us -> 54.1 us  [tap_sum(): jnp.einsum('fhwk,ko->fhwo', window, kernel_part[9 * step_t + 3 * step_h +...]
    unnamed x20 -> x112, local copies, waits for them, and re-layouts: 0.04 us -> 22.8 us
    ppermute x0 -> x30, waiting for transfers between devices: none -> 18.5 us  [the longest x16 18.4 us: gather_around(): earlier.append(lax.ppermute(earlier[-1], axis, up))]
    psum x2, blocking collectives: 67.8 us -> 82.7 us  [moments(): summed, spread = lax.psum((chan_sums, squares), 'height')]
  transfers between devices with their start and end apart: 6 -> 34, of which waited for: 3 -> 4; matrix products, arithmetic and copies ran while one was open for 15% -> 18% of each run, Pallas kernels for 0% -> 0%
where the time goes in v1:
time: 457 us; the launch traced here: 455 us
  starting transfers between devices  197 us (43%)
  blocking collectives  82.7 us (18%)
  waiting for transfers between devices  56 us (12%)
  matrix products  54.1 us (12%)
  other arithmetic  35.6 us (8%)
  local copies, waits for them, and re-layouts  28.8 us (6%)
    ppermute x16, starting transfers between devices, gather_around(): earlier.append(lax.ppermute(earlier[-1], axis, up))  126 us
    psum x2, blocking collectives, moments(): summed, spread = lax.psum((chan_sums, squares), 'height')  82.7 us
    ppermute x14, starting transfers between devices, gather_around(): later.append(lax.ppermute(later[-1], axis, down))  65.3 us
    dot_general x54, matrix products, tap_sum(): jnp.einsum('fhwk,ko->fhwo', window, kernel_part[9 * step_t + 3 * step_h +...  54.1 us
    ppermute x2, waiting for transfers between devices, with_halo(): lax.ppermute(head, axis, [((i + 1) % count, i) for i in range(ends)])  36.4 us
    concatenate x2, other arithmetic, gather_around(): jnp.roll(line, (lax.axis_index(axis) - ways // 2) * x.shape[dim], axis=dim)  31.7 us
    unnamed x112, local copies, waits for them, and re-layouts  22.8 us
    ppermute x16, waiting for transfers between devices, gather_around(): earlier.append(lax.ppermute(earlier[-1], axis, up))  18.4 us
  transfers between devices with their start and end apart: 34, of which 4 were waited for; matrix products, arithmetic and copies ran while one was open for 18% of the time, Pallas kernels for 0%

profile of v1, /device:TPU:0, one launch (start us, length us, event | category | flops | bytes accessed | tf_op | source)
XLA Modules:
  0.0 455.4 jit_solution(3857639946892390162)
XLA Ops:
  0.5 2.6 collective-permute-start.19
  3.1 13.3 %collective-permute-done.2 = bf16[27,32,512]{2,1,0:T(8,128)(2,1)S(1)} collective-permute-done((bf16[27,32,512]{2,1,0:T(8,128)(2,1)}, bf16[27,32,512]{2,1,0:T(8,128)(2,1)S(1)}, u32[]{:S(2)}, u32[]{:S(2)}) %collective-permute-start.2) | collective-permute-done | bytes 884768 | tf_op jit(solution)/shard_map/ppermute | solution.py:15
  16.4 4.4 collective-permute-start.10
  20.9 5.1 %collective-permute-done.19 = bf16[27,32,512]{2,1,0:T(8,128)(2,1)S(1)} collective-permute-done((bf16[27,32,512]{2,1,0:T(8,128)(2,1)}, bf16[27,32,512]{2,1,0:T(8,128)(2,1)S(1)}, u32[]{:S(2)}, u32[]{:S(2)}) %collective-permute-start.19) | collective-permute-done | bytes 884768 | tf_op jit(solution)/shard_map/ppermute | solution.py:15
  26.9 15.9 %collective-permute-start.20 = (bf16[27,32,512]{2,1,0:T(8,128)(2,1)S(1)}, bf16[27,32,512]{2,1,0:T(8,128)(2,1)S(1)}, u32[]{:S(2)}, u32[]{:S(2)}) collective-permute-start(bf16[27,32,512]{2,1,0:T(8,128)(2,1)S(1)} %collective-permute-done.19), channel_id=1, source_target_pairs={{0,1},{1,2},{2,3},{3,4},{4,5},{5,6},{6,7},{7,8},{8,9},{9,10},{10,1... | collective-permute-start | bytes 2654216 | tf_op jit(solution)/shard_map/ppermute | solution.py:15
  42.7 8.5 %collective-permute-start.4 = (bf16[27,32,512]{2,1,0:T(8,128)(2,1)S(1)}, bf16[27,32,512]{2,1,0:T(8,128)(2,1)S(1)}, u32[]{:S(2)}, u32[]{:S(2)}) collective-permute-start(bf16[27,32,512]{2,1,0:T(8,128)(2,1)S(1)} %collective-permute-done.3), channel_id=1, source_target_pairs={{0,1},{1,2},{2,3},{3,4},{4,5},{5,6},{6,7},{7,8},{8,9},{9,10},{10,1... | collective-permute-start | bytes 2654216 | tf_op jit(solution)/shard_map/ppermute | solution.py:15
  51.2 14.0 %collective-permute-start.28 = (bf16[27,32,512]{2,1,0:T(8,128)(2,1)S(1)}, bf16[27,32,512]{2,1,0:T(8,128)(2,1)S(1)}, u32[]{:S(2)}, u32[]{:S(2)}) collective-permute-start(bf16[27,32,512]{2,1,0:T(8,128)(2,1)S(1)} %collective-permute-done.27), channel_id=1, source_target_pairs={{0,15},{1,0},{2,1},{3,2},{4,3},{5,4},{6,5},{7,6},{8,7},{9,8},{10,9... | collective-permute-start | bytes 2654216 | tf_op jit(solution)/shard_map/ppermute | solution.py:17
  65.3 14.3 %collective-permute-start.21 = (bf16[27,32,512]{2,1,0:T(8,128)(2,1)S(1)}, bf16[27,32,512]{2,1,0:T(8,128)(2,1)S(1)}, u32[]{:S(2)}, u32[]{:S(2)}) collective-permute-start(bf16[27,32,512]{2,1,0:T(8,128)(2,1)S(1)} %collective-permute-done.20), channel_id=1, source_target_pairs={{0,1},{1,2},{2,3},{3,4},{4,5},{5,6},{6,7},{7,8},{8,9},{9,10},{10,1... | collective-permute-start | bytes 2654216 | tf_op jit(solution)/shard_map/ppermute | solution.py:15
  79.7 9.5 %collective-permute-start.5 = (bf16[27,32,512]{2,1,0:T(8,128)(2,1)S(1)}, bf16[27,32,512]{2,1,0:T(8,128)(2,1)S(1)}, u32[]{:S(2)}, u32[]{:S(2)}) collective-permute-start(bf16[27,32,512]{2,1,0:T(8,128)(2,1)S(1)} %collective-permute-done.4), channel_id=1, source_target_pairs={{0,1},{1,2},{2,3},{3,4},{4,5},{5,6},{6,7},{7,8},{8,9},{9,10},{10,1... | collective-permute-start | bytes 2654216 | tf_op jit(solution)/shard_map/ppermute | solution.py:15
  89.2 13.9 %collective-permute-start.29 = (bf16[27,32,512]{2,1,0:T(8,128)(2,1)S(1)}, bf16[27,32,512]{2,1,0:T(8,128)(2,1)S(1)}, u32[]{:S(2)}, u32[]{:S(2)}) collective-permute-start(bf16[27,32,512]{2,1,0:T(8,128)(2,1)S(1)} %collective-permute-done.28), channel_id=1, source_target_pairs={{0,15},{1,0},{2,1},{3,2},{4,3},{5,4},{6,5},{7,6},{8,7},{9,8},{10,9... | collective-permute-start | bytes 2654216 | tf_op jit(solution)/shard_map/ppermute | solution.py:17
  103.1 14.5 %collective-permute-start.22 = (bf16[27,32,512]{2,1,0:T(8,128)(2,1)S(1)}, bf16[27,32,512]{2,1,0:T(8,128)(2,1)S(1)}, u32[]{:S(2)}, u32[]{:S(2)}) collective-permute-start(bf16[27,32,512]{2,1,0:T(8,128)(2,1)S(1)} %collective-permute-done.21), channel_id=1, source_target_pairs={{0,1},{1,2},{2,3},{3,4},{4,5},{5,6},{6,7},{7,8},{8,9},{9,10},{10,1... | collective-permute-start | bytes 2654216 | tf_op jit(solution)/shard_map/ppermute | solution.py:15
  117.6 9.5 %collective-permute-start.6 = (bf16[27,32,512]{2,1,0:T(8,128)(2,1)S(1)}, bf16[27,32,512]{2,1,0:T(8,128)(2,1)S(1)}, u32[]{:S(2)}, u32[]{:S(2)}) collective-permute-start(bf16[27,32,512]{2,1,0:T(8,128)(2,1)S(1)} %collective-permute-done.5), channel_id=1, source_target_pairs={{0,1},{1,2},{2,3},{3,4},{4,5},{5,6},{6,7},{7,8},{8,9},{9,10},{10,1... | collective-permute-start | bytes 2654216 | tf_op jit(solution)/shard_map/ppermute | solution.py:15
  127.1 13.9 %collective-permute-start.30 = (bf16[27,32,512]{2,1,0:T(8,128)(2,1)S(1)}, bf16[27,32,512]{2,1,0:T(8,128)(2,1)S(1)}, u32[]{:S(2)}, u32[]{:S(2)}) collective-permute-start(bf16[27,32,512]{2,1,0:T(8,128)(2,1)S(1)} %collective-permute-done.29), channel_id=1, source_target_pairs={{0,15},{1,0},{2,1},{3,2},{4,3},{5,4},{6,5},{7,6},{8,7},{9,8},{10,9... | collective-permute-start | bytes 2654216 | tf_op jit(solution)/shard_map/ppermute | solution.py:17
  141.0 14.5 %collective-permute-start.23 = (bf16[27,32,512]{2,1,0:T(8,128)(2,1)S(1)}, bf16[27,32,512]{2,1,0:T(8,128)(2,1)}, u32[]{:S(2)}, u32[]{:S(2)}) collective-permute-start(bf16[27,32,512]{2,1,0:T(8,128)(2,1)S(1)} %collective-permute-done.22), channel_id=1, source_target_pairs={{0,1},{1,2},{2,3},{3,4},{4,5},{5,6},{6,7},{7,8},{8,9},{9,10},{10,1... | collective-permute-start | bytes 2654216 | tf_op jit(solution)/shard_map/ppermute | solution.py:15
  155.5 9.5 %collective-permute-start.7 = (bf16[27,32,512]{2,1,0:T(8,128)(2,1)S(1)}, bf16[27,32,512]{2,1,0:T(8,128)(2,1)}, u32[]{:S(2)}, u32[]{:S(2)}) collective-permute-start(bf16[27,32,512]{2,1,0:T(8,128)(2,1)S(1)} %collective-permute-done.6), channel_id=1, source_target_pairs={{0,1},{1,2},{2,3},{3,4},{4,5},{5,6},{6,7},{7,8},{8,9},{9,10},{10,1... | collective-permute-start | bytes 2654216 | tf_op jit(solution)/shard_map/ppermute | solution.py:15
  165.0 13.9 %collective-permute-start.31 = (bf16[27,32,512]{2,1,0:T(8,128)(2,1)S(1)}, bf16[27,32,512]{2,1,0:T(8,128)(2,1)S(1)}, u32[]{:S(2)}, u32[]{:S(2)}) collective-permute-start(bf16[27,32,512]{2,1,0:T(8,128)(2,1)S(1)} %collective-permute-done.30), channel_id=1, source_target_pairs={{0,15},{1,0},{2,1},{3,2},{4,3},{5,4},{6,5},{7,6},{8,7},{9,8},{10,9... | collective-permute-start | bytes 2654216 | tf_op jit(solution)/shard_map/ppermute | solution.py:17
  178.9 14.5 %collective-permute-start.24 = (bf16[27,32,512]{2,1,0:T(8,128)(2,1)}, bf16[27,32,512]{2,1,0:T(8,128)(2,1)}, u32[]{:S(2)}, u32[]{:S(2)}) collective-permute-start(bf16[27,32,512]{2,1,0:T(8,128)(2,1)} %collective-permute-done.23), channel_id=1, source_target_pairs={{0,1},{1,2},{2,3},{3,4},{4,5},{5,6},{6,7},{7,8},{8,9},{9,10},{10,1... | collective-permute-start | bytes 2654216 | tf_op jit(solution)/shard_map/ppermute | solution.py:15
  193.4 9.5 %collective-permute-start.8 = (bf16[27,32,512]{2,1,0:T(8,128)(2,1)}, bf16[27,32,512]{2,1,0:T(8,128)(2,1)}, u32[]{:S(2)}, u32[]{:S(2)}) collective-permute-start(bf16[27,32,512]{2,1,0:T(8,128)(2,1)} %collective-permute-done.7), channel_id=1, source_target_pairs={{0,1},{1,2},{2,3},{3,4},{4,5},{5,6},{6,7},{7,8},{8,9},{9,10},{10,1... | collective-permute-start | bytes 2654216 | tf_op jit(solution)/shard_map/ppermute | solution.py:15
  204.5 42.2 %all-reduce.3 = (f32[32]{0:T(128)S(1)}, f32[32]{0:T(128)S(1)}) all-reduce(f32[32]{0:T(128)S(1)} %reduce_sum.75, f32[32]{0:T(128)S(1)} %reduce_sum.73), channel_id=1, replica_groups=mesh['groups'=2,'height'=16] {'height'}, use_global_device_ids=true, to_apply=%region_5.0 | all-reduce | flops 64 | bytes 512 | tf_op jit(solution)/shard_map/psum | solution.py:45
  249.1 1.7 collective-permute-start.9
  250.8 2.0 collective-permute-start
  255.2 36.4 %collective-permute-done.1 = bf16[3,1,80,512]{3,2,1,0:T(8,128)(2,1)S(1)} collective-permute-done((bf16[3,1,80,512]{3,2,1,0:T(8,128)(2,1)S(1)}, bf16[3,1,80,512]{3,2,1,0:T(8,128)(2,1)S(1)}, u32[]{:S(2)}, u32[]{:S(2)}) %collective-permute-start.1) | collective-permute-done | bytes 245792 | tf_op jit(solution)/shard_map/ppermute | solution.py:32
  291.9 2.2 collective-permute-start.16
  294.1 2.6 collective-permute-start.33
  308.6 15.8 %fusion.1 = bf16[27,512,512]{2,1,0:T(8,128)(2,1)S(1)} fusion(s32[]{:T(128)S(6)} %select_n.13, bf16[27,512,512]{2,1,0:T(8,128)(2,1)S(1)} %constant_dynamic-update-slice_fusion), kind=kLoop, calls=%fused_computation.5 | loop fusion | flops 28311552 | bytes 28311556 | tf_op jit(solution)/shard_map/jit(_roll_dynamic)/concatenate | solution.py:19
  335.1 1.5 fusion.92
  344.4 5.5 %convolution_add_fusion.3 = f32[3,2,80,512]{3,2,1,0:T(8,128)S(1)} fusion(bf16[3,2,80,512]{3,2,1,0:T(8,128)(2,1)S(1)} %fusion.30, f32[3,2,80,512]{3,2,1,0:T(8,128)S(1)} %fusion.73, f32[3,2,80,512]{3,2,1,0:T(8,128)S(1)} %fusion.74, f32[3,2,80,512]{3,2,1,0:T(8,128)} %fusion.32, f32[3,2,80,512]{3,2,1,0:T(8,128)S(1)} %fusion.75, ...), kind=kOutput, calls=%fused_computation.26 | convolution fusion | flops 257064960 | bytes 23625728 | tf_op jit(solution)/shard_map/fhwk,ko->fhwo/dot_general | solution.py:76
  351.6 40.5 %all-reduce.2 = (f32[32]{0:T(128)S(1)}, f32[32]{0:T(128)S(1)}) all-reduce(f32[32]{0:T(128)S(1)} %reduce_sum.79, f32[32]{0:T(128)S(1)} %reduce_sum.77), channel_id=1, replica_groups=mesh['groups'=2,'height'=16] {'height'}, use_global_device_ids=true, to_apply=%region_11.13 | all-reduce | flops 64 | bytes 512 | tf_op jit(solution)/shard_map/psum | solution.py:45
  407.2 16.0 %fusion = bf16[27,512,512]{2,1,0:T(8,128)(2,1)S(1)} fusion(s32[]{:T(128)S(6)} %select_n.13, bf16[27,512,512]{2,1,0:T(8,128)(2,1)S(1)} %constant_dynamic-update-slice_fusion.16), kind=kLoop, calls=%fused_computation.4 | loop fusion | flops 28311552 | bytes 28311556 | tf_op jit(solution)/shard_map/jit(_roll_dynamic)/concatenate | solution.py:19
  428.1 1.5 fusion.58
  444.3 5.7 %convolution_add_fusion.1 = f32[3,2,80,512]{3,2,1,0:T(8,128)S(1)} fusion(bf16[3,2,80,512]{3,2,1,0:T(8,128)(2,1)S(1)} %fusion.20, f32[3,2,80,512]{3,2,1,0:T(8,128)} %fusion.50, f32[3,2,80,512]{3,2,1,0:T(8,128)} %fusion.51, f32[3,2,80,512]{3,2,1,0:T(8,128)} %fusion.40, f32[3,2,80,512]{3,2,1,0:T(8,128)} %fusion.52, f32[3,2,80,512]{3,2,1,0:T(8,128)} %fusion.53, ...), kind=kOutput, calls=%fused_computation.20 | convolution fusion | flops 257064960 | bytes 23625728 | tf_op jit(solution)/shard_map/fhwk,ko->fhwo/dot_general | solution.py:76
  453.2 2.2 reshape.33
  (238 shorter events, 77.5 us)
Async XLA Ops:
  0.5 25.5 %collective-permute-start.19 = (bf16[27,32,512]{2,1,0:T(8,128)(2,1)}, bf16[27,32,512]{2,1,0:T(8,128)(2,1)S(1)}, u32[]{:S(2)}, u32[]{:S(2)}) collective-permute-start(bf16[27,32,512]{2,1,0:T(8,128)(2,1)} %param.18), channel_id=1, source_target_pairs={{0,1},{1,2},{2,3},{3,4},{4,5},{5,6},{6,7},{7,8},{8,9},{9,10},{10,1... | collective-permute-start | bytes 2654216 | tf_op jit(solution)/shard_map/ppermute | solution.py:15
  16.4 26.4 %collective-permute-start.3 = (bf16[27,32,512]{2,1,0:T(8,128)(2,1)S(1)}, bf16[27,32,512]{2,1,0:T(8,128)(2,1)S(1)}, u32[]{:S(2)}, u32[]{:S(2)}) collective-permute-start(bf16[27,32,512]{2,1,0:T(8,128)(2,1)S(1)} %collective-permute-done.2), channel_id=1, source_target_pairs={{0,1},{1,2},{2,3},{3,4},{4,5},{5,6},{6,7},{7,8},{8,9},{9,10},{10,1... | collective-permute-start | bytes 2654216 | tf_op jit(solution)/shard_map/ppermute | solution.py:15
  16.4 34.8 %collective-permute-start.10 = (bf16[27,32,512]{2,1,0:T(8,128)(2,1)}, bf16[27,32,512]{2,1,0:T(8,128)(2,1)S(1)}, u32[]{:S(2)}, u32[]{:S(2)}) collective-permute-start(bf16[27,32,512]{2,1,0:T(8,128)(2,1)} %param.14), channel_id=1, source_target_pairs={{0,15},{1,0},{2,1},{3,2},{4,3},{5,4},{6,5},{7,6},{8,7},{9,8},{10,9... | collective-permute-start | bytes 2654216 | tf_op jit(solution)/shard_map/ppermute | solution.py:17
  20.8 30.4 %collective-permute-start.27 = (bf16[27,32,512]{2,1,0:T(8,128)(2,1)}, bf16[27,32,512]{2,1,0:T(8,128)(2,1)S(1)}, u32[]{:S(2)}, u32[]{:S(2)}) collective-permute-start(bf16[27,32,512]{2,1,0:T(8,128)(2,1)} %param.18), channel_id=1, source_target_pairs={{0,15},{1,0},{2,1},{3,2},{4,3},{5,4},{6,5},{7,6},{8,7},{9,8},{10,9... | collective-permute-start | bytes 2654216 | tf_op jit(solution)/shard_map/ppermute | solution.py:17
  26.9 38.4 %collective-permute-start.20 = (bf16[27,32,512]{2,1,0:T(8,128)(2,1)S(1)}, bf16[27,32,512]{2,1,0:T(8,128)(2,1)S(1)}, u32[]{:S(2)}, u32[]{:S(2)}) collective-permute-start(bf16[27,32,512]{2,1,0:T(8,128)(2,1)S(1)} %collective-permute-done.19), channel_id=1, source_target_pairs={{0,1},{1,2},{2,3},{3,4},{4,5},{5,6},{6,7},{7,8},{8,9},{9,10},{10,1... | collective-permute-start | bytes 2654216 | tf_op jit(solution)/shard_map/ppermute | solution.py:15
  42.7 36.9 %collective-permute-start.4 = (bf16[27,32,512]{2,1,0:T(8,128)(2,1)S(1)}, bf16[27,32,512]{2,1,0:T(8,128)(2,1)S(1)}, u32[]{:S(2)}, u32[]{:S(2)}) collective-permute-start(bf16[27,32,512]{2,1,0:T(8,128)(2,1)S(1)} %collective-permute-done.3), channel_id=1, source_target_pairs={{0,1},{1,2},{2,3},{3,4},{4,5},{5,6},{6,7},{7,8},{8,9},{9,10},{10,1... | collective-permute-start | bytes 2654216 | tf_op jit(solution)/shard_map/ppermute | solution.py:15
  51.2 37.9 %collective-permute-start.11 = (bf16[27,32,512]{2,1,0:T(8,128)(2,1)S(1)}, bf16[27,32,512]{2,1,0:T(8,128)(2,1)S(1)}, u32[]{:S(2)}, u32[]{:S(2)}) collective-permute-start(bf16[27,32,512]{2,1,0:T(8,128)(2,1)S(1)} %collective-permute-done.10), channel_id=1, source_target_pairs={{0,15},{1,0},{2,1},{3,2},{4,3},{5,4},{6,5},{7,6},{8,7},{9,8},{10,9... | collective-permute-start | bytes 2654216 | tf_op jit(solution)/shard_map/ppermute | solution.py:17
  51.2 37.9 %collective-permute-start.28 = (bf16[27,32,512]{2,1,0:T(8,128)(2,1)S(1)}, bf16[27,32,512]{2,1,0:T(8,128)(2,1)S(1)}, u32[]{:S(2)}, u32[]{:S(2)}) collective-permute-start(bf16[27,32,512]{2,1,0:T(8,128)(2,1)S(1)} %collective-permute-done.27), channel_id=1, source_target_pairs={{0,15},{1,0},{2,1},{3,2},{4,3},{5,4},{6,5},{7,6},{8,7},{9,8},{10,9... | collective-permute-start | bytes 2654216 | tf_op jit(solution)/shard_map/ppermute | solution.py:17
  65.3 37.8 %collective-permute-start.21 = (bf16[27,32,512]{2,1,0:T(8,128)(2,1)S(1)}, bf16[27,32,512]{2,1,0:T(8,128)(2,1)S(1)}, u32[]{:S(2)}, u32[]{:S(2)}) collective-permute-start(bf16[27,32,512]{2,1,0:T(8,128)(2,1)S(1)} %collective-permute-done.20), channel_id=1, source_target_pairs={{0,1},{1,2},{2,3},{3,4},{4,5},{5,6},{6,7},{7,8},{8,9},{9,10},{10,1... | collective-permute-start | bytes 2654216 | tf_op jit(solution)/shard_map/ppermute | solution.py:15
  79.7 37.9 %collective-permute-start.5 = (bf16[27,32,512]{2,1,0:T(8,128)(2,1)S(1)}, bf16[27,32,512]{2,1,0:T(8,128)(2,1)S(1)}, u32[]{:S(2)}, u32[]{:S(2)}) collective-permute-start(bf16[27,32,512]{2,1,0:T(8,128)(2,1)S(1)} %collective-permute-done.4), channel_id=1, source_target_pairs={{0,1},{1,2},{2,3},{3,4},{4,5},{5,6},{6,7},{7,8},{8,9},{9,10},{10,1... | collective-permute-start | bytes 2654216 | tf_op jit(solution)/shard_map/ppermute | solution.py:15
  89.1 37.9 %collective-permute-start.12 = (bf16[27,32,512]{2,1,0:T(8,128)(2,1)S(1)}, bf16[27,32,512]{2,1,0:T(8,128)(2,1)S(1)}, u32[]{:S(2)}, u32[]{:S(2)}) collective-permute-start(bf16[27,32,512]{2,1,0:T(8,128)(2,1)S(1)} %collective-permute-done.11), channel_id=1, source_target_pairs={{0,15},{1,0},{2,1},{3,2},{4,3},{5,4},{6,5},{7,6},{8,7},{9,8},{10,9... | collective-permute-start | bytes 2654216 | tf_op jit(solution)/shard_map/ppermute | solution.py:17
  89.2 37.9 %collective-permute-start.29 = (bf16[27,32,512]{2,1,0:T(8,128)(2,1)S(1)}, bf16[27,32,512]{2,1,0:T(8,128)(2,1)S(1)}, u32[]{:S(2)}, u32[]{:S(2)}) collective-permute-start(bf16[27,32,512]{2,1,0:T(8,128)(2,1)S(1)} %collective-permute-done.28), channel_id=1, source_target_pairs={{0,15},{1,0},{2,1},{3,2},{4,3},{5,4},{6,5},{7,6},{8,7},{9,8},{10,9... | collective-permute-start | bytes 2654216 | tf_op jit(solution)/shard_map/ppermute | solution.py:17
  103.1 37.9 %collective-permute-start.22 = (bf16[27,32,512]{2,1,0:T(8,128)(2,1)S(1)}, bf16[27,32,512]{2,1,0:T(8,128)(2,1)S(1)}, u32[]{:S(2)}, u32[]{:S(2)}) collective-permute-start(bf16[27,32,512]{2,1,0:T(8,128)(2,1)S(1)} %collective-permute-done.21), channel_id=1, source_target_pairs={{0,1},{1,2},{2,3},{3,4},{4,5},{5,6},{6,7},{7,8},{8,9},{9,10},{10,1... | collective-permute-start | bytes 2654216 | tf_op jit(solution)/shard_map/ppermute | solution.py:15
  117.6 37.9 %collective-permute-start.6 = (bf16[27,32,512]{2,1,0:T(8,128)(2,1)S(1)}, bf16[27,32,512]{2,1,0:T(8,128)(2,1)S(1)}, u32[]{:S(2)}, u32[]{:S(2)}) collective-permute-start(bf16[27,32,512]{2,1,0:T(8,128)(2,1)S(1)} %collective-permute-done.5), channel_id=1, source_target_pairs={{0,1},{1,2},{2,3},{3,4},{4,5},{5,6},{6,7},{7,8},{8,9},{9,10},{10,1... | collective-permute-start | bytes 2654216 | tf_op jit(solution)/shard_map/ppermute | solution.py:15
  127.0 37.9 %collective-permute-start.13 = (bf16[27,32,512]{2,1,0:T(8,128)(2,1)S(1)}, bf16[27,32,512]{2,1,0:T(8,128)(2,1)}, u32[]{:S(2)}, u32[]{:S(2)}) collective-permute-start(bf16[27,32,512]{2,1,0:T(8,128)(2,1)S(1)} %collective-permute-done.12), channel_id=1, source_target_pairs={{0,15},{1,0},{2,1},{3,2},{4,3},{5,4},{6,5},{7,6},{8,7},{9,8},{10,9... | collective-permute-start | bytes 2654216 | tf_op jit(solution)/shard_map/ppermute | solution.py:17
  127.1 37.9 %collective-permute-start.30 = (bf16[27,32,512]{2,1,0:T(8,128)(2,1)S(1)}, bf16[27,32,512]{2,1,0:T(8,128)(2,1)S(1)}, u32[]{:S(2)}, u32[]{:S(2)}) collective-permute-start(bf16[27,32,512]{2,1,0:T(8,128)(2,1)S(1)} %collective-permute-done.29), channel_id=1, source_target_pairs={{0,15},{1,0},{2,1},{3,2},{4,3},{5,4},{6,5},{7,6},{8,7},{9,8},{10,9... | collective-permute-start | bytes 2654216 | tf_op jit(solution)/shard_map/ppermute | solution.py:17
  141.0 37.9 %collective-permute-start.23 = (bf16[27,32,512]{2,1,0:T(8,128)(2,1)S(1)}, bf16[27,32,512]{2,1,0:T(8,128)(2,1)}, u32[]{:S(2)}, u32[]{:S(2)}) collective-permute-start(bf16[27,32,512]{2,1,0:T(8,128)(2,1)S(1)} %collective-permute-done.22), channel_id=1, source_target_pairs={{0,1},{1,2},{2,3},{3,4},{4,5},{5,6},{6,7},{7,8},{8,9},{9,10},{10,1... | collective-permute-start | bytes 2654216 | tf_op jit(solution)/shard_map/ppermute | solution.py:15
  155.5 37.9 %collective-permute-start.7 = (bf16[27,32,512]{2,1,0:T(8,128)(2,1)S(1)}, bf16[27,32,512]{2,1,0:T(8,128)(2,1)}, u32[]{:S(2)}, u32[]{:S(2)}) collective-permute-start(bf16[27,32,512]{2,1,0:T(8,128)(2,1)S(1)} %collective-permute-done.6), channel_id=1, source_target_pairs={{0,1},{1,2},{2,3},{3,4},{4,5},{5,6},{6,7},{7,8},{8,9},{9,10},{10,1... | collective-permute-start | bytes 2654216 | tf_op jit(solution)/shard_map/ppermute | solution.py:15
  165.0 83.5 %collective-permute-start.14 = (bf16[27,32,512]{2,1,0:T(8,128)(2,1)}, bf16[27,32,512]{2,1,0:T(8,128)(2,1)}, u32[]{:S(2)}, u32[]{:S(2)}) collective-permute-start(bf16[27,32,512]{2,1,0:T(8,128)(2,1)} %collective-permute-done.13), channel_id=1, source_target_pairs={{0,15},{1,0},{2,1},{3,2},{4,3},{5,4},{6,5},{7,6},{8,7},{9,8},{10,9... | collective-permute-start | bytes 2654216 | tf_op jit(solution)/shard_map/ppermute | solution.py:17
  165.0 83.5 %collective-permute-start.31 = (bf16[27,32,512]{2,1,0:T(8,128)(2,1)S(1)}, bf16[27,32,512]{2,1,0:T(8,128)(2,1)S(1)}, u32[]{:S(2)}, u32[]{:S(2)}) collective-permute-start(bf16[27,32,512]{2,1,0:T(8,128)(2,1)S(1)} %collective-permute-done.30), channel_id=1, source_target_pairs={{0,15},{1,0},{2,1},{3,2},{4,3},{5,4},{6,5},{7,6},{8,7},{9,8},{10,9... | collective-permute-start | bytes 2654216 | tf_op jit(solution)/shard_map/ppermute | solution.py:17
  178.9 69.7 %collective-permute-start.24 = (bf16[27,32,512]{2,1,0:T(8,128)(2,1)}, bf16[27,32,512]{2,1,0:T(8,128)(2,1)}, u32[]{:S(2)}, u32[]{:S(2)}) collective-permute-start(bf16[27,32,512]{2,1,0:T(8,128)(2,1)} %collective-permute-done.23), channel_id=1, source_target_pairs={{0,1},{1,2},{2,3},{3,4},{4,5},{5,6},{6,7},{7,8},{8,9},{9,10},{10,1... | collective-permute-start | bytes 2654216 | tf_op jit(solution)/shard_map/ppermute | solution.py:15
  193.4 55.7 %collective-permute-start.8 = (bf16[27,32,512]{2,1,0:T(8,128)(2,1)}, bf16[27,32,512]{2,1,0:T(8,128)(2,1)}, u32[]{:S(2)}, u32[]{:S(2)}) collective-permute-start(bf16[27,32,512]{2,1,0:T(8,128)(2,1)} %collective-permute-done.7), channel_id=1, source_target_pairs={{0,1},{1,2},{2,3},{3,4},{4,5},{5,6},{6,7},{7,8},{8,9},{9,10},{10,1... | collective-permute-start | bytes 2654216 | tf_op jit(solution)/shard_map/ppermute | solution.py:15
  248.4 43.5 %collective-permute-start.15 = (bf16[27,32,512]{2,1,0:T(8,128)(2,1)}, bf16[27,32,512]{2,1,0:T(8,128)(2,1)}, u32[]{:S(2)}, u32[]{:S(2)}) collective-permute-start(bf16[27,32,512]{2,1,0:T(8,128)(2,1)} %collective-permute-done.14), channel_id=1, source_target_pairs={{0,15},{1,0},{2,1},{3,2},{4,3},{5,4},{6,5},{7,6},{8,7},{9,8},{10,9... | collective-permute-start | bytes 2654216 | tf_op jit(solution)/shard_map/ppermute | solution.py:17
  248.5 45.6 %collective-permute-start.32 = (bf16[27,32,512]{2,1,0:T(8,128)(2,1)S(1)}, bf16[27,32,512]{2,1,0:T(8,128)(2,1)}, u32[]{:S(2)}, u32[]{:S(2)}) collective-permute-start(bf16[27,32,512]{2,1,0:T(8,128)(2,1)S(1)} %collective-permute-done.31), channel_id=1, source_target_pairs={{0,15},{1,0},{2,1},{3,2},{4,3},{5,4},{6,5},{7,6},{8,7},{9,8},{10,9... | collective-permute-start | bytes 2654216 | tf_op jit(solution)/shard_map/ppermute | solution.py:17
  248.6 48.1 %collective-permute-start.25 = (bf16[27,32,512]{2,1,0:T(8,128)(2,1)}, bf16[27,32,512]{2,1,0:T(8,128)(2,1)}, u32[]{:S(2)}, u32[]{:S(2)}) collective-permute-start(bf16[27,32,512]{2,1,0:T(8,128)(2,1)} %collective-permute-done.24), channel_id=1, source_target_pairs={{0,1},{1,2},{2,3},{3,4},{4,5},{5,6},{6,7},{7,8},{8,9},{9,10},{10,1... | collective-permute-start | bytes 2654216 | tf_op jit(solution)/shard_map/ppermute | solution.py:15
  249.1 48.5 %collective-permute-start.9 = (bf16[27,32,512]{2,1,0:T(8,128)(2,1)}, bf16[27,32,512]{2,1,0:T(8,128)(2,1)}, u32[]{:S(2)}, u32[]{:S(2)}) collective-permute-start(bf16[27,32,512]{2,1,0:T(8,128)(2,1)} %collective-permute-done.8), channel_id=1, source_target_pairs={{0,1},{1,2},{2,3},{3,4},{4,5},{5,6},{6,7},{7,8},{8,9},{9,10},{10,1... | collective-permute-start | bytes 2654216 | tf_op jit(solution)/shard_map/ppermute | solution.py:15
  253.9 37.8 %collective-permute-start.1 = (bf16[3,1,80,512]{3,2,1,0:T(8,128)(2,1)S(1)}, bf16[3,1,80,512]{3,2,1,0:T(8,128)(2,1)S(1)}, u32[]{:S(2)}, u32[]{:S(2)}) collective-permute-start(bf16[3,1,80,512]{3,2,1,0:T(8,128)(2,1)S(1)} %get-tuple-element.17), channel_id=1, source_target_pairs={{1,0},{2,1},{3,2},{4,3},{5,4},{6,5},{7,6},{8,7},{9,8},{10,9},{11,1... | collective-permute-start | bytes 737288 | tf_op jit(solution)/shard_map/ppermute | solution.py:32
  291.9 16.6 %collective-permute-start.16 = (bf16[27,32,512]{2,1,0:T(8,128)(2,1)}, bf16[27,32,512]{2,1,0:T(8,128)(2,1)S(1)}, u32[]{:S(2)}, u32[]{:S(2)}) collective-permute-start(bf16[27,32,512]{2,1,0:T(8,128)(2,1)} %collective-permute-done.15), channel_id=1, source_target_pairs={{0,15},{1,0},{2,1},{3,2},{4,3},{5,4},{6,5},{7,6},{8,7},{9,8},{10,9... | collective-permute-start | bytes 2654216 | tf_op jit(solution)/shard_map/ppermute | solution.py:17
  294.1 111.7 %collective-permute-start.33 = (bf16[27,32,512]{2,1,0:T(8,128)(2,1)}, bf16[27,32,512]{2,1,0:T(8,128)(2,1)}, u32[]{:S(2)}, u32[]{:S(2)}) collective-permute-start(bf16[27,32,512]{2,1,0:T(8,128)(2,1)} %collective-permute-done.32), channel_id=1, source_target_pairs={{0,15},{1,0},{2,1},{3,2},{4,3},{5,4},{6,5},{7,6},{8,7},{9,8},{10,9... | collective-permute-start | bytes 2654216 | tf_op jit(solution)/shard_map/ppermute | solution.py:17
  296.7 98.7 %collective-permute-start.26 = (bf16[27,32,512]{2,1,0:T(8,128)(2,1)}, bf16[27,32,512]{2,1,0:T(8,128)(2,1)}, u32[]{:S(2)}, u32[]{:S(2)}) collective-permute-start(bf16[27,32,512]{2,1,0:T(8,128)(2,1)} %collective-permute-done.25), channel_id=1, source_target_pairs={{0,1},{1,2},{2,3},{3,4},{4,5},{5,6},{6,7},{7,8},{8,9},{9,10},{10,1... | collective-permute-start | bytes 2654216 | tf_op jit(solution)/shard_map/ppermute | solution.py:15
  392.8 30.3 %collective-permute-start.17 = (bf16[3,1,80,512]{3,2,1,0:T(8,128)(2,1)S(1)}, bf16[3,1,80,512]{3,2,1,0:T(8,128)(2,1)S(1)}, u32[]{:S(2)}, u32[]{:S(2)}) collective-permute-start(bf16[3,1,80,512]{3,2,1,0:T(8,128)(2,1)S(1)} %get-tuple-element.14), channel_id=1, source_target_pairs={{0,1},{1,2},{2,3},{3,4},{4,5},{5,6},{6,7},{7,8},{8,9},{9,10},{10,1... | collective-permute-start | bytes 737288 | tf_op jit(solution)/shard_map/ppermute | solution.py:30
  394.1 29.0 %collective-permute-start.18 = (bf16[3,1,80,512]{3,2,1,0:T(8,128)(2,1)S(1)}, bf16[3,1,80,512]{3,2,1,0:T(8,128)(2,1)S(1)}, u32[]{:S(2)}, u32[]{:S(2)}) collective-permute-start(bf16[3,1,80,512]{3,2,1,0:T(8,128)(2,1)S(1)} %get-tuple-element.15), channel_id=1, source_target_pairs={{1,0},{2,1},{3,2},{4,3},{5,4},{6,5},{7,6},{8,7},{9,8},{10,9},{11,1... | collective-permute-start | bytes 737288 | tf_op jit(solution)/shard_map/ppermute | solution.py:32
  (43 other events, 1195.4 us)
